TPU v7x, 128 devices: a whole 4x4x4 slice. The times are simulated.
128 devices in a mesh: leaf: 32 (over z, y, core), blk: 4 (over x).
Axes of the slice: x: 4, y: 4, z: 4, core: 2. Of those that a mesh axis runs over, the one named last changes fastest.
Arguments:
- panels: float32 [4, 262144], P(None, ('leaf', 'blk')), may hold values from 0 to 10, as said below
- panel_dest: int32 [262144, 1], P(('leaf', 'blk')), may hold values from 0 to 127; in each aligned block of 2048 rows (0 to 2047, 2048 to 4095, ...) at most 32 rows name the same one
- proxy_pool: float32 [3, 8192], replicated, may hold values from -0.5 to 1.5
- proxy_index: int32 [32, 2048], P('leaf'), may hold values from 0 to 8191
- omega: bfloat16 [32, 2048, 128], P('leaf', 'blk'), may hold values from -0.125 to 0.125
- merge_maps: float32 [62, 128, 128], replicated, may hold values from -0.5 to 0.5
Outputs:
- leaf_basis: float32 [128, 262144], P(None, ('leaf', 'blk'))
- leaf_factor: float32 [32, 128, 128], P('leaf')
- ancestor_factor: float32 [32, 5, 128, 128], P('leaf')
Inputs may be any that keep to these rules, and one draw needn't show every extreme that they name: panel_dest holds device numbers, leaf index times 4 plus blk index; of the 2048 panels of one device at most 32 go to the same device, and that many do in some device's panels. `panels`: rows 0 to 2 are coordinates in the unit cube, row 3 a positive weight.
All inputs are finite; a program needn't handle non-finite values.
Results may differ from a plain program's by a relative error of at most 0.012.
The roundings to bfloat16 on the way count: a program that leaves them out, or rounds other values in their place, can miss the bound.
Values may be sent and summed in bfloat16 or wider, within the bound.
No kernel may reach another device: no remote copies, remote signals or barrier semaphores. Data moves between devices by JAX's collectives and lax.ppermute only.
A program may use at most 64 MiB of HBM per device.

v0:
```python
import jax
import jax.numpy as jnp
from jax import lax
from jax.sharding import PartitionSpec as P


def from_partner(value, axis, bit):
    mask = 2**bit
    pairs = [(source, source ^ mask) for source in range(lax.axis_size(axis))]
    return lax.ppermute(value, axis, pairs)


def kernel_tile(row_data, points):
    delta_x = row_data[0][:, None] - points[0][None, :]
    delta_y = row_data[1][:, None] - points[1][None, :]
    delta_z = row_data[2][:, None] - points[2][None, :]
    distance = delta_x * delta_x + delta_y * delta_y + delta_z * delta_z
    return (row_data[3][:, None] * lax.rsqrt(distance + 0.0009)).astype(jnp.bfloat16)


def per_device(panels, panel_dest, proxy_pool, proxy_index, omega, merge_maps):
    highest = lax.Precision.HIGHEST
    device_count = lax.axis_size(("leaf", "blk"))
    blk_count = lax.axis_size("blk")
    leaf_count = lax.axis_size("leaf")
    own_panels = panels.shape[1]
    capacity = 2 * own_panels // device_count
    rank_width = omega.shape[2]
    identity = jnp.eye(rank_width, dtype=jnp.float32)
    destination = panel_dest[:, 0]
    one_hot = (destination[:, None] == jnp.arange(device_count, dtype=jnp.int32)[None, :]).astype(
        jnp.int32
    )
    running = jnp.cumsum(one_hot, axis=0)
    slot_index = jnp.sum(running * one_hot, axis=1) - 1
    position = destination * capacity + slot_index
    outgoing = jnp.zeros((4, device_count * capacity), jnp.float32).at[:, position].set(panels)
    received = lax.all_to_all(outgoing, ("leaf", "blk"), split_axis=1, concat_axis=1, tiled=True)
    leaf_proxies = proxy_index[0]
    points = jnp.take(proxy_pool, leaf_proxies, axis=1)
    tile = kernel_tile(received, points)
    sketch = jnp.dot(
        tile,
        lax.all_gather(omega, "blk", axis=1, tiled=True)[0],
        preferred_element_type=jnp.float32,
    )
    gram_part = jnp.dot(sketch.T, sketch, precision=highest)
    gram_sum = lax.psum(gram_part, "blk")
    gram_full = gram_sum / (own_panels * blk_count) + identity
    lower_factor = jnp.linalg.cholesky(gram_full)
    basis_rows = jax.scipy.linalg.solve_triangular(lower_factor, sketch.T, lower=True)
    returned = lax.all_to_all(basis_rows, ("leaf", "blk"), split_axis=1, concat_axis=1, tiled=True)
    leaf_basis = jnp.take(returned, position, axis=1)
    leaf_index = lax.axis_index("leaf")
    levels = leaf_count.bit_length() - 1
    node_gram = gram_full
    ancestors = []
    for level_index in range(levels):
        heap_index = (leaf_count >> level_index) + (leaf_index >> level_index)
        node_map = lax.dynamic_index_in_dim(merge_maps, heap_index - 2, 0, keepdims=False)
        own_term = jnp.dot(
            jnp.dot(node_map.T, node_gram, precision=highest), node_map, precision=highest
        )
        sibling = from_partner(own_term, "leaf", level_index)
        node_gram = (own_term + sibling) * 0.5
        ancestors.append(node_gram)
    ancestor_grams = jnp.stack(ancestors, axis=0)
    ancestor_factor = jnp.linalg.cholesky(ancestor_grams)
    return (leaf_basis, lower_factor[None], ancestor_factor[None])


def solution(mesh):
    placed = (
        P(None, ("leaf", "blk")),
        P(("leaf", "blk"), None),
        P(),
        P("leaf", None),
        P("leaf", "blk", None),
        P(),
    )
    return jax.shard_map(
        per_device,
        mesh=mesh,
        in_specs=placed,
        out_specs=(P(None, ("leaf", "blk")), P("leaf", None, None), P("leaf", None, None, None)),
        check_vma=False,
    )
```

profile of v0, /device:TPU:4, one launch (start us, length us, event | category | flops | bytes accessed | tf_op | source)
XLA Modules:
  0.0 278.7 jit_solution(1367394919315617126)
XLA Ops:
  7.2 0.8 copy.72
  8.0 0.3 fusion.4
  8.4 0.1 broadcast_add_fusion
  8.5 0.3 copy.73
  8.9 0.6 fusion.1
  9.5 0.1 and_reduce_fusion
  9.6 0.4 copy.74
  10.0 6.1 %scatter_custom_fusion = f32[4,4096]{0,1:T(8,128)S(1)} fusion(s32[2048]{0:T(1024)S(1)} %bitcast.100, f32[2048,4]{1,0:T(8,128)S(1)} %copy.74, f32[]{:T(128)} %constant.155.clone.1), kind=kCustom, calls=%fused_computation.12 | custom fusion | bytes 65540 | tf_op jit(solution)/shard_map/scatter | solution.py:37
  16.1 0.8 copy.75
  16.9 0.8 reshape.156
  17.8 10.5 %all-to-all-start = ((f32[128,1,128]{2,1,0:T(1,128)}), f32[128,1,128]{2,1,0:T(1,128)S(1)}, u32[]{:S(2)}, u32[]{:S(2)}) async-start(f32[128,1,128]{2,1,0:T(1,128)} %reshape.156), calls=%async_computation | async-start | bytes 131072 | tf_op jit(solution)/shard_map/all_to_all | solution.py:38
  28.3 0.0 all-reduce.2.cloned.1.call-start
  28.4 2.6 copy.76
  31.0 7.6 %gather_fusion = f32[2048,3]{1,0:T(8,128)S(1)} fusion(f32[3,8192]{0,1:T(8,128)} %copy.76, s32[2048]{0:T(1024)S(1)} %broadcast_clamp_fusion.1), kind=kCustom, calls=%fused_computation | custom fusion | bytes 57344 | tf_op jit(solution)/shard_map/jit(_take)/gather | solution.py:40
  38.7 0.3 select_bitcast_fusion.1
  39.0 1.4 slice_reduce_fusion.2
  40.5 12.0 %all_gather.3 = bf16[1,2048,128]{2,1,0:T(8,128)(2,1)S(1)} all-gather(bf16[1,512,128]{2,1,0:T(8,128)(2,1)S(1)} %copy-done.1), channel_id=1, replica_groups=mesh['leaf'=32,'blk'=4] {'blk'}, dimensions={1}, use_global_device_ids=true | all-gather | bytes 655360 | tf_op jit(solution)/shard_map/all_gather | solution.py:44
  52.5 0.5 broadcast.191
  53.0 0.8 reduce.36
  53.8 0.2 reshape.157
  54.0 0.8 slice_reduce_fusion.6
  54.7 0.1 sub.82
  54.8 0.1 sub.77
  54.9 0.1 sub.72
  55.0 0.1 mul.48
  55.0 13.4 %fusion = f32[4096,128]{1,0:T(8,128)S(1)} fusion(f32[2048]{0:T(1024)S(1)} %get-tuple-element.16, f32[4096]{0:T(1024)S(1)} %sub.82, f32[2048]{0:T(1024)S(1)} %get-tuple-element.17, f32[4096]{0:T(1024)S(1)} %sub.77, f32[2048]{0:T(1024)S(1)} %get-tuple-element.15, f32[4096]{0:T(1024)S(1)} %sub.72, f32[4096]{0:T(1024)S(1)} %mul.48, ...), kind=kOutput, calls=%fused_computation.4 | convolution fusion | flops 2239758336 | bytes 2711552 | tf_op jit(solution)/shard_map/dot_general | solution.py:42
  68.4 4.1 %fusion.58 = f32[128,128]{1,0:T(8,128)} fusion(f32[4096,128]{1,0:T(8,128)S(1)} %fusion), kind=kOutput, calls=%fused_computation.105 | convolution fusion | flops 805306368 | bytes 2162688 | tf_op jit(solution)/shard_map/dot_general | solution.py:47
  72.6 43.0 %all-reduce.2.cloned.1.call-done = f32[128,128]{1,0:T(8,128)} async-done(((f32[128,128]{1,0:T(8,128)}), f32[128,128]{1,0:T(8,128)}) %all-reduce.2.cloned.1.call-update) | async-done | bytes 65552 | tf_op jit(solution)/shard_map/psum | solution.py:48
  115.6 0.9 convert_add_fusion
  116.5 0.1 copy.77
  116.6 0.9 fusion.31
  117.4 0.1 copy.78
  117.5 11.7 %cholesky.30 = f32[128,128]{1,0:T(8,128)S(1)} custom-call(f32[128,128]{1,0:T(8,128)S(1)} %copy.78), custom_call_target="Cholesky" | custom-call | tf_op jit(solution)/shard_map/jit(cholesky)/cholesky | solution.py:50
  129.3 0.6 compare_reduce_fusion.1
  129.9 1.3 fusion.42
  131.2 9.8 %custom-call.11 = f32[1,128,128]{1,2,0:T(8,128)S(1)} custom-call(f32[1,128,128]{2,1,0:T(8,128)S(1)} %get-tuple-element.25), custom_call_target="InvertDiagBlocksLowerTriangular" | custom-call | tf_op jit(solution)/shard_map/jit(_solve_triangular)/triangular_solve | solution.py:51
  141.0 1.2 fusion.29
  142.2 1.1 fusion.27
  143.3 0.3 collective-permute-start
  143.7 3.2 %fusion.9 = f32[128,128,32]{0,2,1:T(8,128)} fusion(f32[128,32,128]{2,1,0:T(8,128)S(1)} %bitcast.92, f32[1,128,128]{1,2,0:T(8,128)S(1)} %custom-call.11), kind=kOutput, calls=%fused_computation.29 | convolution fusion | flops 805306368 | bytes 4259840 | tf_op jit(solution)/shard_map/jit(_solve_triangular)/triangular_solve | solution.py:51
  146.9 9.5 %all-to-all-start.1 = ((f32[128,128,32]{0,2,1:T(8,128)}), f32[128,128,32]{0,2,1:T(8,128)S(1)}, u32[]{:S(2)}, u32[]{:S(2)}) async-start(f32[128,128,32]{0,2,1:T(8,128)} %fusion.9), calls=%async_computation.1 | async-start | bytes 4194304 | tf_op jit(solution)/shard_map/all_to_all | solution.py:52
  156.4 1.1 fusion.25
  157.5 1.1 fusion.23
  158.7 1.5 collective-permute-start.1
  160.2 21.8 %collective-permute-done.1 = f32[128,128]{0,1:T(8,128)S(1)} collective-permute-done((f32[128,128]{0,1:T(8,128)S(1)}, f32[128,128]{0,1:T(8,128)S(1)}, u32[]{:S(2)}, u32[]{:S(2)}) %collective-permute-start.1) | collective-permute-done | bytes 65568 | tf_op jit(solution)/shard_map/ppermute | solution.py:10
  182.1 1.1 fusion.21
  183.2 1.1 fusion.19
  184.3 2.8 %collective-permute-start.2 = (f32[128,128]{0,1:T(8,128)S(1)}, f32[128,128]{0,1:T(8,128)S(1)}, u32[]{:S(2)}, u32[]{:S(2)}) collective-permute-start(f32[128,128]{0,1:T(8,128)S(1)} %fusion.19), channel_id=1, source_target_pairs={{0,16},{4,20},{8,24},{12,28},{16,0},{20,4},{24,8},{28,12},{32,48},... | collective-permute-start | bytes 196616 | tf_op jit(solution)/shard_map/ppermute | solution.py:10
  187.2 3.0 %collective-permute-done.2 = f32[128,128]{0,1:T(8,128)S(1)} collective-permute-done((f32[128,128]{0,1:T(8,128)S(1)}, f32[128,128]{0,1:T(8,128)S(1)}, u32[]{:S(2)}, u32[]{:S(2)}) %collective-permute-start.2) | collective-permute-done | bytes 65568 | tf_op jit(solution)/shard_map/ppermute | solution.py:10
  190.2 1.1 fusion.17
  191.3 1.1 fusion.15
  192.5 1.8 collective-permute-start.3
  194.2 2.6 collective-permute-done.3
  196.8 1.1 fusion.13
  197.9 1.1 fusion.11
  199.1 3.5 %collective-permute-start.4 = (f32[128,128]{0,1:T(8,128)S(1)}, f32[128,128]{0,1:T(8,128)S(1)}, u32[]{:S(2)}, u32[]{:S(2)}) collective-permute-start(f32[128,128]{0,1:T(8,128)S(1)} %fusion.11), channel_id=1, source_target_pairs={{0,64},{4,68},{8,72},{12,76},{16,80},{20,84},{24,88},{28,92},{32,9... | collective-permute-start | bytes 196616 | tf_op jit(solution)/shard_map/ppermute | solution.py:10
  202.6 2.3 collective-permute-done.4
  205.0 0.2 copy.92
  205.2 58.6 %custom-call.12 = f32[5,128,128]{2,1,0:T(8,128)S(1)} custom-call(f32[5,128,128]{2,1,0:T(8,128)S(1)} %fusion.8), custom_call_target="Cholesky" | custom-call | tf_op jit(solution)/shard_map/jit(cholesky)/cholesky | solution.py:68
  263.8 0.1 compare_reduce_fusion
  263.9 0.8 select_bitcast_fusion.2
  264.8 5.5 %gather_fusion.1 = f32[2048,128]{1,0:T(8,128)S(1)} fusion(f32[128,4096]{0,1:T(8,128)S(1)} %bitcast.91, s32[2048]{0:T(1024)S(1)} %broadcast_clamp_fusion), kind=kCustom, calls=%fused_computation.1 | custom fusion | bytes 2105344 | tf_op jit(solution)/shard_map/jit(_take)/gather | solution.py:53
  270.2 0.3 select_bitcast_fusion
  270.6 1.3 copy.93
  (32 shorter events, 0.3 us)
Async XLA Ops:
  7.2 1.7 copy-start.2
  7.2 2.4 copy-start.3
  8.9 19.5 %copy-start = (f32[3,8192]{1,0:T(4,128)S(1)}, f32[3,8192]{1,0:T(4,128)}, u32[]{:S(2)}) copy-start(f32[3,8192]{1,0:T(4,128)} %param.8) | copy-start | bytes 294916
  16.1 14.9 %copy-start.4 = (s32[1,2048]{1,0:T(1,128)S(1)}, s32[1,2048]{1,0:T(1,128)}, u32[]{:S(2)}) copy-start(s32[1,2048]{1,0:T(1,128)} %param.9) | copy-start | bytes 24580
  17.8 34.7 %all-to-all-start = ((f32[128,1,128]{2,1,0:T(1,128)}), f32[128,1,128]{2,1,0:T(1,128)S(1)}, u32[]{:S(2)}, u32[]{:S(2)}) async-start(f32[128,1,128]{2,1,0:T(1,128)} %reshape.156), calls=%async_computation | async-start | bytes 131072 | tf_op jit(solution)/shard_map/all_to_all | solution.py:38
  28.3 87.4 %all-reduce.2.cloned.1.call-start = ((), (), s32[]{:S(2)}) async-start(), calls=%async_computation.2 | async-start | bytes 131072 | tf_op jit(solution)/shard_map/psum | solution.py:48
  28.3 12.1 %copy-start.1 = (bf16[1,512,128]{2,1,0:T(8,128)(2,1)S(1)}, bf16[1,512,128]{2,1,0:T(8,128)(2,1)}, u32[]{:S(2)}) copy-start(bf16[1,512,128]{2,1,0:T(8,128)(2,1)} %param.10) | copy-start | bytes 393220
  143.3 13.1 %collective-permute-start = (f32[128,128]{0,1:T(8,128)S(1)}, f32[128,128]{0,1:T(8,128)S(1)}, u32[]{:S(2)}, u32[]{:S(2)}) collective-permute-start(f32[128,128]{0,1:T(8,128)S(1)} %fusion.27), channel_id=1, source_target_pairs={{0,4},{4,0},{8,12},{12,8},{16,20},{20,16},{24,28},{28,24},{32,36},... | collective-permute-start | bytes 196616 | tf_op jit(solution)/shard_map/ppermute | solution.py:10
  146.9 117.9 %all-to-all-start.1 = ((f32[128,128,32]{0,2,1:T(8,128)}), f32[128,128,32]{0,2,1:T(8,128)S(1)}, u32[]{:S(2)}, u32[]{:S(2)}) async-start(f32[128,128,32]{0,2,1:T(8,128)} %fusion.9), calls=%async_computation.1 | async-start | bytes 4194304 | tf_op jit(solution)/shard_map/all_to_all | solution.py:52
  158.7 23.4 %collective-permute-start.1 = (f32[128,128]{0,1:T(8,128)S(1)}, f32[128,128]{0,1:T(8,128)S(1)}, u32[]{:S(2)}, u32[]{:S(2)}) collective-permute-start(f32[128,128]{0,1:T(8,128)S(1)} %fusion.23), channel_id=1, source_target_pairs={{0,8},{4,12},{8,0},{12,4},{16,24},{20,28},{24,16},{28,20},{32,40},... | collective-permute-start | bytes 196616 | tf_op jit(solution)/shard_map/ppermute | solution.py:10
  184.3 5.8 %collective-permute-start.2 = (f32[128,128]{0,1:T(8,128)S(1)}, f32[128,128]{0,1:T(8,128)S(1)}, u32[]{:S(2)}, u32[]{:S(2)}) collective-permute-start(f32[128,128]{0,1:T(8,128)S(1)} %fusion.19), channel_id=1, source_target_pairs={{0,16},{4,20},{8,24},{12,28},{16,0},{20,4},{24,8},{28,12},{32,48},... | collective-permute-start | bytes 196616 | tf_op jit(solution)/shard_map/ppermute | solution.py:10
  192.5 4.3 %collective-permute-start.3 = (f32[128,128]{0,1:T(8,128)S(1)}, f32[128,128]{0,1:T(8,128)S(1)}, u32[]{:S(2)}, u32[]{:S(2)}) collective-permute-start(f32[128,128]{0,1:T(8,128)S(1)} %fusion.15), channel_id=1, source_target_pairs={{0,32},{4,36},{8,40},{12,44},{16,48},{20,52},{24,56},{28,60},{32,0... | collective-permute-start | bytes 196616 | tf_op jit(solution)/shard_map/ppermute | solution.py:10
  199.1 5.8 %collective-permute-start.4 = (f32[128,128]{0,1:T(8,128)S(1)}, f32[128,128]{0,1:T(8,128)S(1)}, u32[]{:S(2)}, u32[]{:S(2)}) collective-permute-start(f32[128,128]{0,1:T(8,128)S(1)} %fusion.11), channel_id=1, source_target_pairs={{0,64},{4,68},{8,72},{12,76},{16,80},{20,84},{24,88},{28,92},{32,9... | collective-permute-start | bytes 196616 | tf_op jit(solution)/shard_map/ppermute | solution.py:10
Sparse Core Ops, SparseCore 0:
  72.7 42.9 all-reduce.1
where the time goes:
time: 280 us; the launch traced here: 279 us
  other arithmetic  87.6 us (31%)
  waiting for transfers between devices  72.8 us (26%)
  matrix products  32 us (11%)
  starting transfers between devices  30.1 us (11%)
  local copies, waits for them, and re-layouts  29.9 us (11%)
  between operations  14.5 us (5%)
  blocking collectives  12 us (4%)
    another operation x3, other arithmetic, per_device(): ancestor_factor = jnp.linalg.cholesky(ancestor_grams)  58.8 us
    psum x1, waiting for transfers between devices, per_device(): gram_sum = lax.psum(gram_part, 'blk')  43 us
    ppermute x5, waiting for transfers between devices, from_partner(): return lax.ppermute(value, axis, pairs)  29.7 us
    dot_general x1, matrix products, per_device(): jnp.dot(tile, lax.all_gather(omega, 'blk', axis=1, tiled=True)[0], prefer...  13.4 us
    another operation x4, other arithmetic, per_device(): lower_factor = jnp.linalg.cholesky(gram_full)  12.4 us
    all_gather x1, blocking collectives, per_device(): lax.all_gather(omega, 'blk', axis=1, tiled=True)[0]  12 us
    all_to_all x1, starting transfers between devices, per_device(): lax.all_to_all(outgoing, ('leaf', 'blk'), split_axis=1, concat_axis=1, ti...  10.5 us
    ppermute x5, starting transfers between devices, from_partner(): return lax.ppermute(value, axis, pairs)  10 us
  transfers between devices with their start and end apart: 8, of which 5 were waited for; matrix products, arithmetic and copies ran while one was open for 30% of the time, Pallas kernels for 0%

commit v1 on v0

--- a/solution.py
+++ b/solution.py
@@ -1,12 +1,22 @@
+import functools
+
 import jax
 import jax.numpy as jnp
 from jax import lax
+from jax.experimental import pallas as pl
+from jax.experimental.pallas import tpu as pltpu
 from jax.sharding import PartitionSpec as P
 
 
 def from_partner(value, axis, bit):
     mask = 2**bit
     pairs = [(source, source ^ mask) for source in range(lax.axis_size(axis))]
+    return lax.ppermute(value, axis, pairs)
+
+
+def from_shift(value, axis, shift):
+    size = lax.axis_size(axis)
+    pairs = [(source, (source + shift) % size) for source in range(size)]
     return lax.ppermute(value, axis, pairs)
 
 
@@ -18,15 +28,71 @@
     return (row_data[3][:, None] * lax.rsqrt(distance + 0.0009)).astype(jnp.bfloat16)
 
 
+def _cholesky_body(with_inverse, a_ref, l_ref, *rest):
+    if with_inverse:
+        inv_ref, work, inverse_work = rest
+    else:
+        (work,) = rest
+    count, n, _ = a_ref.shape
+    rows = lax.broadcasted_iota(jnp.int32, (n, n), 0)
+    cols = lax.broadcasted_iota(jnp.int32, (n, n), 1)
+    sub = lax.broadcasted_iota(jnp.int32, (n, 1), 0)
+    lane = lax.broadcasted_iota(jnp.int32, (1, n), 1)
+    work[...] = a_ref[...]
+    if with_inverse:
+        eye = jnp.where(rows == cols, 1.0, 0.0).astype(jnp.float32)
+        for b in range(count):
+            inverse_work[b] = eye
+
+    def step(j, carry):
+        for b in range(count):
+            full = work[b]
+            row = work[b, pl.ds(j, 1), :]
+            pivot = jnp.sum(jnp.where(lane == j, row, 0.0), axis=1, keepdims=True)
+            scale = lax.rsqrt(pivot)
+            column = jnp.sum(jnp.where(cols == j, full, 0.0), axis=1, keepdims=True)
+            factor = jnp.where(sub > j, column / pivot, 0.0)
+            work[b] = jnp.where(sub == j, row * scale, full - factor * row)
+            if with_inverse:
+                inverse_full = inverse_work[b]
+                inverse_row = inverse_work[b, pl.ds(j, 1), :]
+                inverse_work[b] = jnp.where(
+                    sub == j, inverse_row * scale, inverse_full - factor * inverse_row
+                )
+        return carry
+
+    lax.fori_loop(0, n, step, 0)
+    for b in range(count):
+        l_ref[b] = jnp.transpose(jnp.where(cols >= rows, work[b], 0.0))
+        if with_inverse:
+            inv_ref[b] = jnp.where(cols <= rows, inverse_work[b], 0.0)
+
+
+def cholesky_batch(a, with_inverse):
+    count, n, _ = a.shape
+    shape = jax.ShapeDtypeStruct((count, n, n), jnp.float32)
+    vmem = pl.BlockSpec(memory_space=pltpu.VMEM)
+    scratch = [pltpu.VMEM((count, n, n), jnp.float32)] * (2 if with_inverse else 1)
+    return pl.pallas_call(
+        functools.partial(_cholesky_body, with_inverse),
+        out_shape=(shape, shape) if with_inverse else shape,
+        in_specs=[vmem],
+        out_specs=(vmem, vmem) if with_inverse else vmem,
+        scratch_shapes=scratch,
+    )(a)
+
+
 def per_device(panels, panel_dest, proxy_pool, proxy_index, omega, merge_maps):
     highest = lax.Precision.HIGHEST
     device_count = lax.axis_size(("leaf", "blk"))
     blk_count = lax.axis_size("blk")
     leaf_count = lax.axis_size("leaf")
+    blk_index = lax.axis_index("blk")
     own_panels = panels.shape[1]
     capacity = 2 * own_panels // device_count
     rank_width = omega.shape[2]
     identity = jnp.eye(rank_width, dtype=jnp.float32)
+    omega_parts = [omega[0]] + [from_shift(omega[0], "blk", shift) for shift in range(1, blk_count)]
     destination = panel_dest[:, 0]
     one_hot = (destination[:, None] == jnp.arange(device_count, dtype=jnp.int32)[None, :]).astype(
         jnp.int32
@@ -39,18 +105,22 @@
     leaf_proxies = proxy_index[0]
     points = jnp.take(proxy_pool, leaf_proxies, axis=1)
     tile = kernel_tile(received, points)
-    sketch = jnp.dot(
-        tile,
-        lax.all_gather(omega, "blk", axis=1, tiled=True)[0],
-        preferred_element_type=jnp.float32,
+    chunk = omega.shape[1]
+    sketch = jnp.zeros((received.shape[1], rank_width), jnp.float32)
+    for shift in range(blk_count):
+        source = (blk_index - shift) % blk_count
+        part = lax.dynamic_slice_in_dim(tile, source * chunk, chunk, 1)
+        sketch = sketch + jnp.dot(part, omega_parts[shift], preferred_element_type=jnp.float32)
+    gram_part = jnp.dot(sketch.T, sketch, precision=highest)
+    gram_sum = gram_part + from_partner(gram_part, "blk", 0)
+    gram_sum = gram_sum + from_partner(gram_sum, "blk", 1)
+    gram_full = gram_sum / (own_panels * blk_count) + identity
+    lower_factor, lower_inverse = cholesky_batch(gram_full[None], True)
+    basis_rows = jnp.dot(lower_inverse[0], sketch.T, precision=highest)
+    returned = lax.all_to_all(
+        basis_rows.astype(jnp.bfloat16), ("leaf", "blk"), split_axis=1, concat_axis=1, tiled=True
     )
-    gram_part = jnp.dot(sketch.T, sketch, precision=highest)
-    gram_sum = lax.psum(gram_part, "blk")
-    gram_full = gram_sum / (own_panels * blk_count) + identity
-    lower_factor = jnp.linalg.cholesky(gram_full)
-    basis_rows = jax.scipy.linalg.solve_triangular(lower_factor, sketch.T, lower=True)
-    returned = lax.all_to_all(basis_rows, ("leaf", "blk"), split_axis=1, concat_axis=1, tiled=True)
-    leaf_basis = jnp.take(returned, position, axis=1)
+    leaf_basis = jnp.take(returned, position, axis=1).astype(jnp.float32)
     leaf_index = lax.axis_index("leaf")
     levels = leaf_count.bit_length() - 1
     node_gram = gram_full
@@ -65,8 +135,8 @@
         node_gram = (own_term + sibling) * 0.5
         ancestors.append(node_gram)
     ancestor_grams = jnp.stack(ancestors, axis=0)
-    ancestor_factor = jnp.linalg.cholesky(ancestor_grams)
-    return (leaf_basis, lower_factor[None], ancestor_factor[None])
+    ancestor_factor = cholesky_batch(ancestor_grams, False)
+    return (leaf_basis, lower_factor, ancestor_factor[None])
 
 
 def solution(mesh):

time: 280 us -> 222 us (0.79)
  Pallas kernels: 0 us -> 82.5 us
  other arithmetic: 87.6 us -> 19.9 us
  waiting for transfers between devices: 72.8 us -> 26.4 us
  between operations: 14.5 us -> 1.12 us
  blocking collectives: 12 us -> 0 us
  matrix products: 32 us -> 22.2 us
  starting transfers between devices: 30.1 us -> 36.3 us
  local copies, waits for them, and re-layouts: 29.9 us -> 33.1 us
    pallas_call x0 -> x2, Pallas kernels: none -> 82.5 us  [cholesky_batch(): pl.pallas_call(functools.partial(_cholesky_body, with_inverse), out_shape...]
    another operation x12 -> x3, other arithmetic: 81.4 us -> 0.45 us  [the longest x3 58.8 us: per_device(): ancestor_factor = jnp.linalg.cholesky(ancestor_grams)]
    psum x1 -> x0, waiting for transfers between devices: 43 us -> none  [per_device(): gram_sum = lax.psum(gram_part, 'blk')]
    convert_element_type x0 -> x2, other arithmetic: none -> 16.9 us  [the longest x1 16.5 us: kernel_tile(): (row_data[3][:, None] * lax.rsqrt(distance + 0.0009)).astype(jnp.bfloat16)]
    all_gather x1 -> x0, blocking collectives: 12 us -> none  [per_device(): lax.all_gather(omega, 'blk', axis=1, tiled=True)[0]]
    dot_general x1 -> x5, matrix products: 13.4 us -> 7.84 us  [the longest x4 5.06 us: per_device(): jnp.dot(part, omega_parts[shift], preferred_element_type=jnp.float32)]
    ppermute x0 -> x3, starting transfers between devices: none -> 3.73 us  [from_shift(): return lax.ppermute(value, axis, pairs)]
    ppermute x5 -> x7, waiting for transfers between devices: 29.7 us -> 26.3 us  [from_partner(): return lax.ppermute(value, axis, pairs)]
  transfers between devices with their start and end apart: 8 -> 12, of which waited for: 5 -> 6; matrix products, arithmetic and copies ran while one was open for 30% -> 27% of each run, Pallas kernels for 0% -> 37%
where the time goes in v1:
time: 222 us; the launch traced here: 221 us
  Pallas kernels  82.5 us (37%)
  starting transfers between devices  36.3 us (16%)
  local copies, waits for them, and re-layouts  33.1 us (15%)
  waiting for transfers between devices  26.4 us (12%)
  matrix products  22.2 us (10%)
  other arithmetic  19.9 us (9%)
    pallas_call x2, Pallas kernels, cholesky_batch(): pl.pallas_call(functools.partial(_cholesky_body, with_inverse), out_shape...  82.5 us
    ppermute x7, waiting for transfers between devices, from_partner(): return lax.ppermute(value, axis, pairs)  26.3 us
    convert_element_type x1, other arithmetic, kernel_tile(): (row_data[3][:, None] * lax.rsqrt(distance + 0.0009)).astype(jnp.bfloat16)  16.5 us
    ppermute x7, starting transfers between devices, from_partner(): return lax.ppermute(value, axis, pairs)  12.2 us
    all_to_all x1, starting transfers between devices, per_device(): lax.all_to_all(outgoing, ('leaf', 'blk'), split_axis=1, concat_axis=1, ti...  10.6 us
    all_to_all x1, starting transfers between devices, per_device(): lax.all_to_all(basis_rows.astype(jnp.bfloat16), ('leaf', 'blk'), split_ax...  9.87 us
    gather x1, local copies, waits for them, and re-layouts, per_device(): points = jnp.take(proxy_pool, leaf_proxies, axis=1)  7.65 us
    unnamed x15, local copies, waits for them, and re-layouts  6.83 us
  transfers between devices with their start and end apart: 12, of which 6 were waited for; matrix products, arithmetic and copies ran while one was open for 27% of the time, Pallas kernels for 37%

profile of v1, /device:TPU:4, one launch (start us, length us, event | category | flops | bytes accessed | tf_op | source)
XLA Modules:
  0.0 221.4 jit_solution(5220615565281009299)
XLA Ops:
  0.6 1.3 collective-permute-start
  1.9 0.8 collective-permute-start.2
  2.7 1.6 collective-permute-start.1
  4.4 0.8 copy.21
  5.2 0.3 fusion.10
  5.6 0.1 broadcast_add_fusion
  5.6 0.3 copy.22
  6.0 0.6 fusion.7
  6.7 0.4 copy.23
  7.1 6.1 %scatter_custom_fusion = f32[4,4096]{0,1:T(8,128)S(1)} fusion(s32[2048]{0:T(1024)S(1)} %bitcast.93, f32[2048,4]{1,0:T(8,128)S(1)} %copy.23, f32[]{:T(128)} %constant.109.clone.1), kind=kCustom, calls=%fused_computation.21 | custom fusion | bytes 65540 | tf_op jit(solution)/shard_map/scatter | solution.py:103
  13.2 0.8 copy.24
  14.0 0.8 reshape.139
  14.9 10.6 %all-to-all-start = ((f32[128,1,128]{2,1,0:T(1,128)}), f32[128,1,128]{2,1,0:T(1,128)S(1)}, u32[]{:S(2)}, u32[]{:S(2)}) async-start(f32[128,1,128]{2,1,0:T(1,128)} %reshape.139), calls=%async_computation | async-start | bytes 131072 | tf_op jit(solution)/shard_map/all_to_all | solution.py:104
  25.5 3.4 %copy.25 = f32[3,8192]{0,1:T(8,128)} copy(f32[3,8192]{1,0:T(4,128)} %param.8) | data formatting | bytes 196608 | tf_op args[2]
  28.9 7.6 %gather_fusion = f32[2048,3]{1,0:T(8,128)S(1)} fusion(f32[3,8192]{0,1:T(8,128)} %copy.25, s32[2048]{0:T(1024)S(1)} %broadcast_clamp_fusion.1), kind=kCustom, calls=%fused_computation | custom fusion | bytes 57344 | tf_op jit(solution)/shard_map/jit(_take)/gather | solution.py:106
  36.6 0.3 select_bitcast_fusion
  36.9 1.4 slice_reduce_fusion.2
  38.5 0.5 broadcast.127
  39.0 0.8 reduce.24
  39.8 0.2 reshape.140
  40.0 0.8 slice_reduce_fusion.6
  40.7 0.1 mul.60
  40.8 0.1 sub.81
  40.9 0.1 sub.86
  41.0 0.1 sub.91
  41.1 16.5 %multiply_convert_fusion = bf16[4096,2048]{1,0:T(8,128)(2,1)S(1)} fusion(f32[2048]{0:T(1024)S(1)} %get-tuple-element.17, f32[4096]{0:T(1024)S(1)} %sub.91, f32[2048]{0:T(1024)S(1)} %get-tuple-element.18, f32[4096]{0:T(1024)S(1)} %sub.86, f32[2048]{0:T(1024)S(1)} %get-tuple-element.16, f32[4096]{0:T(1024)S(1)} %sub.81, f32[4096]{0:T(1024)S(1)} %mul.60), kind=kLoop, calls=%fused_computation.3 | loop fusion | flops 92274688 | bytes 16867328 | tf_op jit(solution)/shard_map/convert_element_type | solution.py:28
  57.6 1.3 fusion.5
  58.9 1.3 convolution_add_fusion.1
  60.2 1.3 fusion.1
  61.5 1.3 fusion
  62.7 3.5 %fusion.65 = f32[128,128]{1,0:T(8,128)S(1)} fusion(f32[4096,128]{1,0:T(8,128)S(1)} %fusion), kind=kOutput, calls=%fused_computation.105 | convolution fusion | flops 805306368 | bytes 2162688 | tf_op jit(solution)/shard_map/dot_general | solution.py:114
  66.2 1.3 collective-permute-start.3
  67.4 3.1 %collective-permute-done.3 = f32[128,128]{1,0:T(8,128)S(1)} collective-permute-done((f32[128,128]{1,0:T(8,128)S(1)}, f32[128,128]{1,0:T(8,128)S(1)}, u32[]{:S(2)}, u32[]{:S(2)}) %collective-permute-start.3) | collective-permute-done | bytes 65568 | tf_op jit(solution)/shard_map/ppermute | solution.py:14
  70.5 1.1 collective-permute-start.4
  71.7 4.7 %collective-permute-done.4 = f32[128,128]{1,0:T(8,128)S(1)} collective-permute-done((f32[128,128]{1,0:T(8,128)S(1)}, f32[128,128]{1,0:T(8,128)S(1)}, u32[]{:S(2)}, u32[]{:S(2)}) %collective-permute-start.4) | collective-permute-done | bytes 65568 | tf_op jit(solution)/shard_map/ppermute | solution.py:14
  76.4 1.1 fusion.31
  77.5 1.0 fusion.29
  78.6 0.1 collective-permute-start.5
  78.7 0.6 fusion.44.a_ref
  79.3 15.5 %shard_map.85 = (f32[1,128,128]{2,1,0:T(8,128)}, f32[1,128,128]{2,1,0:T(8,128)}) custom-call(f32[1,128,128]{2,1,0:T(8,128)} %fusion.44.a_ref), custom_call_target="tpu_custom_call" | custom-call | tf_op jit(solution)/shard_map/pallas_call | solution.py:76
  94.8 2.8 %convolution_convert_fusion = bf16[128,4096]{1,0:T(8,128)(2,1)S(1)} fusion(f32[4096,128]{1,0:T(8,128)S(1)} %fusion, f32[1,128,128]{2,1,0:T(8,128)} %get-tuple-element.5), kind=kOutput, calls=%fused_computation.7 | convolution fusion | flops 805830656 | bytes 3211264 | tf_op jit(solution)/shard_map/dot_general | solution.py:119
  97.6 1.3 copy.26
  98.9 9.9 %all-to-all-start.1 = ((bf16[128,128,32]{0,2,1:T(8,128)(2,1)}), bf16[128,128,32]{0,2,1:T(8,128)(2,1)S(1)}, u32[]{:S(2)}, u32[]{:S(2)}) async-start(bf16[128,128,32]{0,2,1:T(8,128)(2,1)} %bitcast.16), calls=%async_computation.1 | async-start | bytes 2097152 | tf_op jit(solution)/shard_map/all_to_all | solution.py:120
  108.8 1.1 fusion.27
  109.9 1.0 fusion.25
  111.0 1.5 collective-permute-start.6
  112.6 10.7 %collective-permute-done.6 = f32[128,128]{1,0:T(8,128)S(1)} collective-permute-done((f32[128,128]{1,0:T(8,128)S(1)}, f32[128,128]{1,0:T(8,128)S(1)}, u32[]{:S(2)}, u32[]{:S(2)}) %collective-permute-start.6) | collective-permute-done | bytes 65568 | tf_op jit(solution)/shard_map/ppermute | solution.py:14
  123.2 1.1 fusion.23
  124.4 1.0 fusion.21
  125.4 2.8 %collective-permute-start.7 = (f32[128,128]{1,0:T(8,128)S(1)}, f32[128,128]{1,0:T(8,128)S(1)}, u32[]{:S(2)}, u32[]{:S(2)}) collective-permute-start(f32[128,128]{1,0:T(8,128)S(1)} %fusion.21), channel_id=1, source_target_pairs={{0,16},{4,20},{8,24},{12,28},{16,0},{20,4},{24,8},{28,12},{32,48},... | collective-permute-start | bytes 196616 | tf_op jit(solution)/shard_map/ppermute | solution.py:14
  128.3 3.0 %collective-permute-done.7 = f32[128,128]{1,0:T(8,128)S(1)} collective-permute-done((f32[128,128]{1,0:T(8,128)S(1)}, f32[128,128]{1,0:T(8,128)S(1)}, u32[]{:S(2)}, u32[]{:S(2)}) %collective-permute-start.7) | collective-permute-done | bytes 65568 | tf_op jit(solution)/shard_map/ppermute | solution.py:14
  131.3 1.1 fusion.19
  132.4 1.0 fusion.17
  133.5 1.8 collective-permute-start.8
  135.2 2.6 %collective-permute-done.8 = f32[128,128]{1,0:T(8,128)S(1)} collective-permute-done((f32[128,128]{1,0:T(8,128)S(1)}, f32[128,128]{1,0:T(8,128)S(1)}, u32[]{:S(2)}, u32[]{:S(2)}) %collective-permute-start.8) | collective-permute-done | bytes 65568 | tf_op jit(solution)/shard_map/ppermute | solution.py:14
  137.8 1.1 fusion.15
  138.9 1.0 fusion.13
  140.0 3.5 %collective-permute-start.9 = (f32[128,128]{1,0:T(8,128)S(1)}, f32[128,128]{1,0:T(8,128)S(1)}, u32[]{:S(2)}, u32[]{:S(2)}) collective-permute-start(f32[128,128]{1,0:T(8,128)S(1)} %fusion.13), channel_id=1, source_target_pairs={{0,64},{4,68},{8,72},{12,76},{16,80},{20,84},{24,88},{28,92},{32,9... | collective-permute-start | bytes 196616 | tf_op jit(solution)/shard_map/ppermute | solution.py:14
  143.6 2.3 %collective-permute-done.9 = f32[128,128]{1,0:T(8,128)S(1)} collective-permute-done((f32[128,128]{1,0:T(8,128)S(1)}, f32[128,128]{1,0:T(8,128)S(1)}, u32[]{:S(2)}, u32[]{:S(2)}) %collective-permute-start.9) | collective-permute-done | bytes 65568 | tf_op jit(solution)/shard_map/ppermute | solution.py:14
  145.9 0.7 copy-done
  146.6 66.9 %shard_map.86 = f32[5,128,128]{2,1,0:T(8,128)} custom-call(f32[5,128,128]{2,1,0:T(8,128)} %copy-done), custom_call_target="tpu_custom_call" | custom-call | tf_op jit(solution)/shard_map/pallas_call | solution.py:76
  213.5 6.2 %gather_fusion.1 = bf16[2048,128]{1,0:T(8,128)(2,1)S(1)} fusion(bf16[128,4096]{0,1:T(8,128)(2,1)S(1)} %bitcast.81, s32[2048]{0:T(1024)S(1)} %broadcast_clamp_fusion), kind=kCustom, calls=%fused_computation.1 | custom fusion | bytes 1056768 | tf_op jit(solution)/shard_map/jit(_take)/gather | solution.py:123
  219.7 0.3 convert_bitcast_fusion
  220.1 1.3 copy.27
  (30 shorter events, 0.2 us)
Async XLA Ops:
  0.6 5.4 %copy-start.2 = (s32[2048,1]{0,1:T(1,128)S(1)}, s32[2048,1]{0,1:T(1,128)}, u32[]{:S(2)}) copy-start(s32[2048,1]{0,1:T(1,128)} %param.7) | copy-start | bytes 24580
  0.6 6.1 %copy-start.3 = (f32[4,2048]{1,0:T(4,128)S(1)}, f32[4,2048]{1,0:T(4,128)}, u32[]{:S(2)}) copy-start(f32[4,2048]{1,0:T(4,128)} %param.6) | copy-start | bytes 98308
  0.6 58.2 %collective-permute-start = (bf16[512,128]{1,0:T(8,128)(2,1)}, bf16[512,128]{1,0:T(8,128)(2,1)S(1)}, u32[]{:S(2)}, u32[]{:S(2)}) collective-permute-start(bf16[512,128]{1,0:T(8,128)(2,1)} %bitcast.86), channel_id=1, source_target_pairs={{0,1},{1,2},{2,3},{3,0},{4,5},{5,6},{6,7},{7,4},{8,9},{9,10},{10,1... | collective-permute-start | bytes 393224 | tf_op jit(solution)/shard_map/ppermute | solution.py:20
  1.9 58.3 %collective-permute-start.2 = (bf16[512,128]{1,0:T(8,128)(2,1)}, bf16[512,128]{1,0:T(8,128)(2,1)S(1)}, u32[]{:S(2)}, u32[]{:S(2)}) collective-permute-start(bf16[512,128]{1,0:T(8,128)(2,1)} %bitcast.87), channel_id=1, source_target_pairs={{0,3},{1,0},{2,1},{3,2},{4,7},{5,4},{6,5},{7,6},{8,11},{9,8},{10,9... | collective-permute-start | bytes 393224 | tf_op jit(solution)/shard_map/ppermute | solution.py:20
  2.7 58.7 %collective-permute-start.1 = (bf16[512,128]{1,0:T(8,128)(2,1)}, bf16[512,128]{1,0:T(8,128)(2,1)S(1)}, u32[]{:S(2)}, u32[]{:S(2)}) collective-permute-start(bf16[512,128]{1,0:T(8,128)(2,1)} %bitcast.88), channel_id=1, source_target_pairs={{0,2},{1,3},{2,0},{3,1},{4,6},{5,7},{6,4},{7,5},{8,10},{9,11},{10,... | collective-permute-start | bytes 393224 | tf_op jit(solution)/shard_map/ppermute | solution.py:20
  13.2 15.7 %copy-start.4 = (s32[1,2048]{1,0:T(1,128)S(1)}, s32[1,2048]{1,0:T(1,128)}, u32[]{:S(2)}) copy-start(s32[1,2048]{1,0:T(1,128)} %param.9) | copy-start | bytes 24580
  14.9 23.6 %all-to-all-start = ((f32[128,1,128]{2,1,0:T(1,128)}), f32[128,1,128]{2,1,0:T(1,128)S(1)}, u32[]{:S(2)}, u32[]{:S(2)}) async-start(f32[128,1,128]{2,1,0:T(1,128)} %reshape.139), calls=%async_computation | async-start | bytes 131072 | tf_op jit(solution)/shard_map/all_to_all | solution.py:104
  41.1 16.5 %copy-start.1 = (bf16[1,512,128]{2,1,0:T(8,128)(2,1)S(1)}, bf16[1,512,128]{2,1,0:T(8,128)(2,1)}, u32[]{:S(2)}) copy-start(bf16[1,512,128]{2,1,0:T(8,128)(2,1)} %param.10) | copy-start | bytes 393220
  66.2 4.3 %collective-permute-start.3 = (f32[128,128]{1,0:T(8,128)S(1)}, f32[128,128]{1,0:T(8,128)S(1)}, u32[]{:S(2)}, u32[]{:S(2)}) collective-permute-start(f32[128,128]{1,0:T(8,128)S(1)} %fusion.65), channel_id=1, source_target_pairs={{0,1},{1,0},{2,3},{3,2},{4,5},{5,4},{6,7},{7,6},{8,9},{9,8},{10,11... | collective-permute-start | bytes 196616 | tf_op jit(solution)/shard_map/ppermute | solution.py:14
  70.5 5.8 %collective-permute-start.4 = (f32[128,128]{1,0:T(8,128)S(1)}, f32[128,128]{1,0:T(8,128)S(1)}, u32[]{:S(2)}, u32[]{:S(2)}) collective-permute-start(f32[128,128]{1,0:T(8,128)S(1)} %add.185), channel_id=1, source_target_pairs={{0,2},{1,3},{2,0},{3,1},{4,6},{5,7},{6,4},{7,5},{8,10},{9,11},{10,... | collective-permute-start | bytes 196616 | tf_op jit(solution)/shard_map/ppermute | solution.py:14
  78.6 30.2 %collective-permute-start.5 = (f32[128,128]{1,0:T(8,128)S(1)}, f32[128,128]{1,0:T(8,128)S(1)}, u32[]{:S(2)}, u32[]{:S(2)}) collective-permute-start(f32[128,128]{1,0:T(8,128)S(1)} %fusion.29), channel_id=1, source_target_pairs={{0,4},{4,0},{8,12},{12,8},{16,20},{20,16},{24,28},{28,24},{32,36},... | collective-permute-start | bytes 196616 | tf_op jit(solution)/shard_map/ppermute | solution.py:14
  98.9 114.6 %all-to-all-start.1 = ((bf16[128,128,32]{0,2,1:T(8,128)(2,1)}), bf16[128,128,32]{0,2,1:T(8,128)(2,1)S(1)}, u32[]{:S(2)}, u32[]{:S(2)}) async-start(bf16[128,128,32]{0,2,1:T(8,128)(2,1)} %bitcast.16), calls=%async_computation.1 | async-start | bytes 2097152 | tf_op jit(solution)/shard_map/all_to_all | solution.py:120
  111.0 12.2 %collective-permute-start.6 = (f32[128,128]{1,0:T(8,128)S(1)}, f32[128,128]{1,0:T(8,128)S(1)}, u32[]{:S(2)}, u32[]{:S(2)}) collective-permute-start(f32[128,128]{1,0:T(8,128)S(1)} %fusion.25), channel_id=1, source_target_pairs={{0,8},{4,12},{8,0},{12,4},{16,24},{20,28},{24,16},{28,20},{32,40},... | collective-permute-start | bytes 196616 | tf_op jit(solution)/shard_map/ppermute | solution.py:14
  125.4 5.8 %collective-permute-start.7 = (f32[128,128]{1,0:T(8,128)S(1)}, f32[128,128]{1,0:T(8,128)S(1)}, u32[]{:S(2)}, u32[]{:S(2)}) collective-permute-start(f32[128,128]{1,0:T(8,128)S(1)} %fusion.21), channel_id=1, source_target_pairs={{0,16},{4,20},{8,24},{12,28},{16,0},{20,4},{24,8},{28,12},{32,48},... | collective-permute-start | bytes 196616 | tf_op jit(solution)/shard_map/ppermute | solution.py:14
  133.5 4.3 %collective-permute-start.8 = (f32[128,128]{1,0:T(8,128)S(1)}, f32[128,128]{1,0:T(8,128)S(1)}, u32[]{:S(2)}, u32[]{:S(2)}) collective-permute-start(f32[128,128]{1,0:T(8,128)S(1)} %fusion.17), channel_id=1, source_target_pairs={{0,32},{4,36},{8,40},{12,44},{16,48},{20,52},{24,56},{28,60},{32,0... | collective-permute-start | bytes 196616 | tf_op jit(solution)/shard_map/ppermute | solution.py:14
  140.0 5.8 %collective-permute-start.9 = (f32[128,128]{1,0:T(8,128)S(1)}, f32[128,128]{1,0:T(8,128)S(1)}, u32[]{:S(2)}, u32[]{:S(2)}) collective-permute-start(f32[128,128]{1,0:T(8,128)S(1)} %fusion.13), channel_id=1, source_target_pairs={{0,64},{4,68},{8,72},{12,76},{16,80},{20,84},{24,88},{28,92},{32,9... | collective-permute-start | bytes 196616 | tf_op jit(solution)/shard_map/ppermute | solution.py:14
  145.9 0.7 copy-start
